TPU v7x, 256 devices: a whole 4x4x8 slice. The times are simulated.
256 devices in a mesh: expert: 32 (over x, z), tensor: 8 (over y, core).
Axes of the slice: x: 4, y: 4, z: 8, core: 2. Of those that a mesh axis runs over, the one named last changes fastest.
Arguments:
- attn_vals: bfloat16 [2048, 4096], P('expert', 'tensor'), may hold values from -6 to 6
- residual: bfloat16 [2048, 4096], P('expert', 'tensor'), may hold values from -6 to 6
- out_weight: bfloat16 [4096, 4096], P('tensor'), may hold values from -0.09375 to 0.09375
- norm_gain: float32 [4096], P('tensor'), may hold values from 0.5 to 1.5
- router_weight: float32 [4096, 8], P('tensor'), may hold values from -0.09375 to 0.09375
- routes: int32 [2048, 2], P('expert'), may hold values from 0 to 7, all different within a row; in each aligned block of 64 rows (0 to 63, 64 to 127, ...) at most 32 rows name the same one
- w_gate: bfloat16 [32, 4096, 2048], P('expert', None, 'tensor'), may hold values from -0.09375 to 0.09375
- w_up: bfloat16 [32, 4096, 2048], P('expert', None, 'tensor'), may hold values from -0.09375 to 0.09375
- w_down: bfloat16 [32, 2048, 4096], P('expert', 'tensor'), may hold values from -0.0625 to 0.0625
- slab_of: int32 [32], replicated, may hold values from 0 to 31, each once
- final_gain: float32 [4096], P('tensor'), may hold values from 0.5 to 1.5
- row_order: int32 [2048], replicated, may hold values from 0 to 2047, each once
Outputs:
- stream_out: bfloat16 [2048, 4096], P('expert', 'tensor')
- normed_out: bfloat16 [2048, 4096], P('expert', 'tensor')
Inputs may be any that keep to these rules, and one draw needn't show every extreme that they name: `routes`: the two experts of a row differ. In each aligned block of 64 rows (the rows of one device) no expert is named by more than 32 rows, and some block names one expert exactly 32 times. `slab_of`: A permutation. `row_order`: A permutation.
All inputs are finite; a program needn't handle non-finite values.
Results may differ from a plain program's by a relative error of at most 0.017.
Values may be sent and summed in bfloat16 or wider, within the bound.
No kernel may reach another device: no remote copies, remote signals or barrier semaphores. Data moves between devices by JAX's collectives and lax.ppermute only.
A program may use at most 128 MiB of HBM per device.

v0:
```python
import jax
import jax.numpy as jnp
from jax import lax
from jax.sharding import PartitionSpec as P

D = 4096
MOST = 32
EPS = 1e-05


def finish_slots(gate_val, up_val, down_weight):
    active = (jax.nn.silu(gate_val) * up_val).astype(jnp.bfloat16)
    partial_out = jnp.einsum("gmf,fd->gmd", active, down_weight, preferred_element_type=jnp.float32)
    summed = lax.psum_scatter(
        partial_out.astype(jnp.bfloat16), "tensor", scatter_dimension=2, tiled=True
    )
    return lax.all_to_all(summed, "expert", split_axis=0, concat_axis=0, tiled=True)


def final_norm(stream, final_gain):
    stream_f = stream.astype(jnp.float32)
    square_total = lax.psum(jnp.sum(stream_f * stream_f, axis=1), "tensor")
    factor = lax.rsqrt(square_total / D + EPS)
    return (stream_f * factor[:, None] * final_gain).astype(jnp.bfloat16)


def on_device(
    attn_vals,
    residual,
    out_weight,
    norm_gain,
    router_weight,
    routes,
    w_gate,
    w_up,
    w_down,
    slab_of,
    final_gain,
    row_order,
):
    groups = lax.axis_size("expert")
    row_count = attn_vals.shape[0]
    expert_count = router_weight.shape[1]
    slab_count = groups // expert_count
    partial_proj = jnp.dot(attn_vals, out_weight, preferred_element_type=jnp.float32)
    project = lax.psum_scatter(
        partial_proj.astype(jnp.bfloat16), "tensor", scatter_dimension=1, tiled=True
    ).astype(jnp.float32)
    stream_in = (residual.astype(jnp.float32) + project).astype(jnp.bfloat16)
    hidden_f = stream_in.astype(jnp.float32)
    scaled = hidden_f * norm_gain
    square_sum, logit_part = lax.psum(
        (
            jnp.sum(hidden_f * hidden_f, axis=1),
            jnp.dot(scaled, router_weight, precision=lax.Precision.HIGHEST),
        ),
        "tensor",
    )
    inverse_rms = lax.rsqrt(square_sum / D + EPS)
    normed_in = (scaled * inverse_rms[:, None]).astype(jnp.bfloat16)
    logits = logit_part * inverse_rms[:, None]
    expert_ids = jnp.arange(expert_count, dtype=jnp.int32)
    route_hot = (routes[:, :, None] == expert_ids[None, None, :]).astype(jnp.int32)
    chosen = jnp.sum(route_hot.astype(jnp.float32) * logits[:, None, :], axis=2)
    leading = jax.nn.sigmoid(chosen[:, 0] - chosen[:, 1])
    mixing = jnp.stack([leading, 1.0 - leading], axis=1)
    route_hits = jnp.sum(route_hot, axis=1)
    before_count = jnp.cumsum(route_hits, axis=0) - route_hits
    slot_ids = jnp.sum(route_hot * before_count[:, None, :], axis=2)
    slot_hot = (slot_ids[:, :, None] == jnp.arange(MOST, dtype=jnp.int32)[None, None, :]).astype(
        jnp.float32
    )
    placing = jnp.einsum("rke,rks->esr", route_hot.astype(jnp.float32), slot_hot).astype(
        jnp.bfloat16
    )
    target_expert = slab_of // slab_count
    send_map = jnp.take(placing, target_expert, axis=0)
    outgoing = jnp.einsum(
        "gsr,rd->gsd", send_map, normed_in, preferred_element_type=jnp.float32
    ).astype(jnp.bfloat16)
    arrived_part = lax.all_to_all(outgoing, "expert", split_axis=0, concat_axis=0, tiled=True)
    arrived = lax.all_gather(arrived_part, "tensor", axis=2, tiled=True)
    gate_val = jnp.einsum("gmd,df->gmf", arrived, w_gate[0], preferred_element_type=jnp.float32)
    up_val = jnp.einsum("gmd,df->gmf", arrived, w_up[0], preferred_element_type=jnp.float32)
    returned = finish_slots(gate_val, up_val, w_down[0])
    group_ids = jnp.arange(groups, dtype=jnp.int32)
    holder_hot = (slab_of[None, :] == group_ids[:, None]).astype(jnp.int32)
    holders = jnp.sum(holder_hot * group_ids[None, :], axis=1).reshape(expert_count, slab_count)
    row_holders = jnp.take(holders, routes, axis=0)
    flat_index = row_holders * MOST + slot_ids[:, :, None]
    flat_back = returned.reshape(groups * MOST, returned.shape[2])
    fetched = jnp.take(flat_back, flat_index.reshape(-1), axis=0).reshape(
        row_count, 2, slab_count, returned.shape[2]
    )
    expert_out = jnp.sum(fetched.astype(jnp.float32), axis=2)
    blended = jnp.sum(mixing[:, :, None] * expert_out, axis=1)
    stream = (hidden_f + blended).astype(jnp.bfloat16)
    positions = lax.axis_index("expert") * row_count + jnp.arange(row_count, dtype=jnp.int32)
    matches = (row_order[None, :] == positions[:, None]).astype(jnp.int32)
    source = jnp.sum(matches * jnp.arange(row_order.shape[0], dtype=jnp.int32)[None, :], axis=1)
    all_stream = lax.all_gather(stream, "expert", axis=0, tiled=True)
    ordered = jnp.take(all_stream, source, axis=0)
    return (ordered, final_norm(ordered, final_gain))


def solution(mesh):
    return jax.shard_map(
        on_device,
        mesh=mesh,
        in_specs=(
            P("expert", "tensor"),
            P("expert", "tensor"),
            P("tensor", None),
            P("tensor"),
            P("tensor", None),
            P("expert", None),
            P("expert", None, "tensor"),
            P("expert", None, "tensor"),
            P("expert", "tensor", None),
            P(),
            P("tensor"),
            P(),
        ),
        out_specs=(P("expert", "tensor"), P("expert", "tensor")),
        check_vma=False,
    )
```

profile of v0, /device:TPU:1, one launch (start us, length us, event | category | flops | bytes accessed | tf_op | source)
XLA Modules:
  0.0 367.0 jit_solution(5263027604369193061)
XLA Ops:
  7.2 4.0 %convolution_convert_fusion.1 = bf16[64,4096]{1,0:T(8,128)(2,1)} fusion(bf16[64,512]{1,0:T(8,128)(2,1)} %param.12, bf16[512,4096]{1,0:T(8,128)(2,1)} %param.14), kind=kOutput, calls=%fused_computation.5 | convolution fusion | flops 268697600 | bytes 4784128 | tf_op jit(solution)/shard_map/dot_general | solution.py:45
  11.4 0.2 convert_reduce_fusion.1
  11.7 1.2 select_reduce_fusion.1
  12.9 0.4 fusion.13
  13.6 0.6 gather_fusion.1
  14.2 32.7 %reduce-scatter.3.cloned.1.call-done = bf16[64,512]{1,0:T(8,128)(2,1)} async-done(((bf16[64,4096]{1,0:T(8,128)(2,1)}), bf16[64,512]{1,0:T(8,128)(2,1)}) %reduce-scatter.3.cloned.1.call-update) | async-done | bytes 65552 | tf_op jit(solution)/shard_map/reduce_scatter | solution.py:46
  46.8 1.0 fusion.28
  47.8 0.2 fusion.23
  48.0 14.9 %all-reduce = (f32[64]{0:T(128)S(1)}, f32[64,8]{0,1:T(8,128)S(1)}) all-reduce(f32[64]{0:T(128)S(1)} %get-tuple-element.10, f32[64,8]{0,1:T(8,128)S(1)} %fusion.23), channel_id=1, replica_groups=mesh['expert'=32,'tensor'=8] {'tensor'}, use_global_device_ids=true, to_apply=%region_4.0 | all-reduce | flops 576 | bytes 4608 | tf_op jit(solution)/shard_map/psum | solution.py:52
  62.9 0.5 convolution_convert_fusion.2
  63.4 34.6 %all_to_all.10 = bf16[32,32,512]{2,1,0:T(8,128)(2,1)} all-to-all(bf16[32,32,512]{2,1,0:T(8,128)(2,1)S(1)} %convolution_convert_fusion.2), channel_id=1, replica_groups=mesh['expert'=32,'tensor'=8] {'expert'}, dimensions={0} | all-to-all | bytes 2097152 | tf_op jit(solution)/shard_map/all_to_all | solution.py:81
  98.1 50.6 %all-gather.3.cloned.1.call-done = bf16[32,32,4096]{2,1,0:T(8,128)(2,1)} async-done(((bf16[32,32,512]{2,1,0:T(8,128)(2,1)}), bf16[32,32,4096]{2,1,0:T(8,128)(2,1)}) %all-gather.3.cloned.1.call-update) | async-done | bytes 8388624 | tf_op jit(solution)/shard_map/all_gather | solution.py:82
  148.7 6.3 %fusion.3 = f32[32,32,256]{2,1,0:T(8,128)S(1)} fusion(bf16[32,32,4096]{2,1,0:T(8,128)(2,1)} %all-gather.3.cloned.1.call-done, bf16[1,4096,256]{2,1,0:T(8,128)(2,1)} %param.18), kind=kOutput, calls=%fused_computation.9 | convolution fusion | flops 2147483648 | bytes 11534336 | tf_op jit(solution)/shard_map/gmd,df->gmf/dot_general | solution.py:83
  155.0 16.8 %convolution_convert_fusion = bf16[32,32,4096]{2,1,0:T(8,128)(2,1)} fusion(bf16[1,256,4096]{2,1,0:T(8,128)(2,1)S(1)} %copy-done, bf16[32,32,4096]{2,1,0:T(8,128)(2,1)} %all-gather.3.cloned.1.call-done, bf16[1,4096,256]{2,1,0:T(8,128)(2,1)} %param.19, f32[32,32,256]{2,1,0:T(8,128)S(1)} %fusion.3), kind=kOutput, calls=%fused_computation.4 | convolution fusion | flops 4300734464 | bytes 22020096 | tf_op jit(solution)/shard_map/gmf,fd->gmd/dot_general | solution.py:13
  171.8 54.4 %reduce-scatter.5.cloned.1.call-done = bf16[32,32,512]{2,1,0:T(8,128)(2,1)} async-done(((bf16[32,32,4096]{2,1,0:T(8,128)(2,1)}), bf16[32,32,512]{2,1,0:T(8,128)(2,1)}) %reduce-scatter.5.cloned.1.call-update) | async-done | bytes 1048592 | tf_op jit(solution)/shard_map/reduce_scatter | solution.py:14
  226.2 9.5 %all-to-all-start.1 = ((bf16[32,32,512]{2,1,0:T(8,128)(2,1)}), bf16[32,32,512]{2,1,0:T(8,128)(2,1)S(1)}, u32[]{:S(2)}, u32[]{:S(2)}) async-start(bf16[32,32,512]{2,1,0:T(8,128)(2,1)} %reduce-scatter.5.cloned.1.call-done), calls=%async_computation.3 | async-start | bytes 2097152 | tf_op jit(solution)/shard_map/all_to_all | solution.py:17
  235.8 0.2 all-gather.5.cloned.1.call-start
  236.2 0.1 reshape.129
  236.6 0.6 gather_fusion
  237.9 0.2 fusion.33
  238.4 22.5 %all-to-all-done.1 = bf16[32,32,512]{2,1,0:T(8,128)(2,1)S(1)} async-done(((bf16[32,32,512]{2,1,0:T(8,128)(2,1)}), bf16[32,32,512]{2,1,0:T(8,128)(2,1)S(1)}, u32[]{:S(2)}, u32[]{:S(2)}) %all-to-all-start.1) | async-done | bytes 1048608 | tf_op jit(solution)/shard_map/all_to_all | solution.py:17
  261.0 2.6 gather_fusion.2
  263.6 1.2 gather.21
  264.8 0.9 convert_reduce_fusion
  265.7 0.4 multiply_reduce_fusion
  266.1 0.6 fusion.29
  266.8 0.2 select_reduce_fusion
  267.1 72.8 %all-gather.5.cloned.1.call-done = bf16[2048,512]{1,0:T(8,128)(2,1)} async-done(((bf16[64,512]{1,0:T(8,128)(2,1)}), bf16[2048,512]{1,0:T(8,128)(2,1)}) %all-gather.5.cloned.1.call-update) | async-done | bytes 2097168 | tf_op jit(solution)/shard_map/all_gather | solution.py:101
  339.9 2.6 gather_fusion.3
  342.5 0.2 fusion.25
  342.7 17.1 %psum.23 = f32[64]{0:T(128)S(1)} all-reduce(f32[64]{0:T(128)S(1)} %get-tuple-element.4), channel_id=1, replica_groups=mesh['expert'=32,'tensor'=8] {'tensor'}, use_global_device_ids=true, to_apply=%region_14.15 | all-reduce | flops 64 | bytes 512 | tf_op jit(solution)/shard_map/psum | solution.py:22
  359.7 0.7 fusion.27
  (59 shorter events, 2.0 us)
Async XLA Ops:
  7.2 147.8 %copy-start = (bf16[1,256,4096]{2,1,0:T(8,128)(2,1)S(1)}, bf16[1,256,4096]{2,1,0:T(8,128)(2,1)}, u32[]{:S(2)}) copy-start(bf16[1,256,4096]{2,1,0:T(8,128)(2,1)} %param.20) | copy-start | bytes 6291460
  7.2 4.1 %copy-start.6 = (s32[64,2]{0,1:T(2,128)S(1)}, s32[64,2]{0,1:T(2,128)}, u32[]{:S(2)}) copy-start(s32[64,2]{0,1:T(2,128)} %param.17) | copy-start | bytes 1540
  7.2 39.6 %reduce-scatter.3.cloned.1.call-start = ((), (), s32[]{:S(2)}) async-start(), calls=%async_computation.4 | async-start | bytes 589824 | tf_op jit(solution)/shard_map/reduce_scatter | solution.py:46
  11.2 2.3 copy-start.8
  11.2 35.6 %copy-start.2 = (bf16[64,512]{1,0:T(8,128)(2,1)S(1)}, bf16[64,512]{1,0:T(8,128)(2,1)}, u32[]{:S(2)}) copy-start(bf16[64,512]{1,0:T(8,128)(2,1)} %param.13) | copy-start | bytes 196612
  11.2 36.6 %copy-start.3 = (f32[512,8]{0,1:T(8,128)S(1)}, f32[512,8]{0,1:T(8,128)}, u32[]{:S(2)}) copy-start(f32[512,8]{0,1:T(8,128)} %param.16) | copy-start | bytes 49156
  11.2 36.6 %copy-start.4 = (f32[512]{0:T(512)S(1)}, f32[512]{0:T(512)}, u32[]{:S(2)}) copy-start(f32[512]{0:T(512)} %param.15) | copy-start | bytes 6148
  11.3 137.4 %all-gather.3.cloned.1.call-start = ((), (), s32[]{:S(2)}) async-start(), calls=%async_computation.5 | async-start | bytes 9437184 | tf_op jit(solution)/shard_map/all_gather | solution.py:82
  98.0 128.2 %reduce-scatter.5.cloned.1.call-start = ((), (), s32[]{:S(2)}) async-start(), calls=%async_computation.6 | async-start | bytes 9437184 | tf_op jit(solution)/shard_map/reduce_scatter | solution.py:14
  226.2 34.7 %all-to-all-start.1 = ((bf16[32,32,512]{2,1,0:T(8,128)(2,1)}), bf16[32,32,512]{2,1,0:T(8,128)(2,1)S(1)}, u32[]{:S(2)}, u32[]{:S(2)}) async-start(bf16[32,32,512]{2,1,0:T(8,128)(2,1)} %reduce-scatter.5.cloned.1.call-done), calls=%async_computation.3 | async-start | bytes 2097152 | tf_op jit(solution)/shard_map/all_to_all | solution.py:17
  235.8 104.1 %all-gather.5.cloned.1.call-start = ((), (), s32[]{:S(2)}) async-start(), calls=%async_computation.7 | async-start | bytes 2162688 | tf_op jit(solution)/shard_map/all_gather | solution.py:101
  263.6 3.2 copy-start.5
  263.6 96.2 %copy-start.7 = (f32[512]{0:T(512)S(1)}, f32[512]{0:T(512)}, u32[]{:S(2)}) copy-start(f32[512]{0:T(512)} %param.22) | copy-start | bytes 6148
  342.6 17.8 %copy-start.1 = (bf16[64,512]{1,0:T(8,128)(2,1)}, bf16[64,512]{1,0:T(8,128)(2,1)S(1)}, u32[]{:S(2)}) copy-start(bf16[64,512]{1,0:T(8,128)(2,1)S(1)} %get-tuple-element.5) | copy-start | bytes 196612
Sparse Core Ops, SparseCore 0:
  11.4 35.4 reduce-scatter.2
  98.1 50.5 all-gather.2
  172.0 54.2 reduce-scatter.4
  266.9 72.9 all-gather.4
where the time goes:
time: 367 us
  waiting for transfers between devices  233 us (63%)
  blocking collectives  66.5 us (18%)
  matrix products  28.2 us (8%)
  between operations  14.1 us (4%)
  starting transfers between devices  9.88 us (3%)
  local copies, waits for them, and re-layouts  9.17 us (2%)
  other arithmetic  6.03 us (2%)
    all_gather x1, waiting for transfers between devices, on_device(): all_stream = lax.all_gather(stream, 'expert', axis=0, tiled=True)  72.8 us
    reduce_scatter x1, waiting for transfers between devices, finish_slots(): lax.psum_scatter(partial_out.astype(jnp.bfloat16), 'tensor', scatter_dime...  54.4 us
    all_gather x1, waiting for transfers between devices, on_device(): arrived = lax.all_gather(arrived_part, 'tensor', axis=2, tiled=True)  50.6 us
    all_to_all x1, blocking collectives, on_device(): lax.all_to_all(outgoing, 'expert', split_axis=0, concat_axis=0, tiled=True)  34.6 us
    reduce_scatter x1, waiting for transfers between devices, on_device(): lax.psum_scatter(partial_proj.astype(jnp.bfloat16), 'tensor', scatter_dim...  32.7 us
    all_to_all x1, waiting for transfers between devices, finish_slots(): lax.all_to_all(summed, 'expert', split_axis=0, concat_axis=0, tiled=True)  22.5 us
    psum x1, blocking collectives, final_norm(): square_total = lax.psum(jnp.sum(stream_f * stream_f, axis=1), 'tensor')  17.1 us
    dot_general x1, matrix products, finish_slots(): jnp.einsum('gmf,fd->gmd', active, down_weight, preferred_element_type=jnp...  16.8 us
  transfers between devices with their start and end apart: 5, of which 5 were waited for; matrix products, arithmetic and copies ran while one was open for 1% of the time, Pallas kernels for 0%

commit v1 on v0

--- a/solution.py
+++ b/solution.py
@@ -6,6 +6,28 @@
 D = 4096
 MOST = 32
 EPS = 1e-05
+
+
+def joined_along(tiles, dim):
+    tiles = jnp.moveaxis(tiles, 0, dim)
+    lengths = tiles.shape
+    return tiles.reshape(*lengths[:dim], lengths[dim] * lengths[dim + 1], *lengths[dim + 2 :])
+
+
+def ring_gather(x, axis, dim):
+    length = lax.axis_size(axis)
+    pairs = [(i, (i + 1) % length) for i in range(length)]
+    back = [(b, a) for a, b in pairs]
+    lower, upper = ([], [])
+    for hop in range(length - 1):
+        if hop % 2 == 0:
+            lower.append(lax.ppermute(lower[-1] if lower else x, axis, pairs))
+        else:
+            upper.append(lax.ppermute(upper[-1] if upper else x, axis, back))
+    blocks = jnp.stack([*lower[::-1], x, *upper])
+    shift = lax.axis_index(axis) - len(lower)
+    blocks = blocks[(jnp.arange(length) - shift) % length]
+    return joined_along(blocks, dim)
 
 
 def finish_slots(gate_val, up_val, down_weight):
@@ -79,7 +101,7 @@
         "gsr,rd->gsd", send_map, normed_in, preferred_element_type=jnp.float32
     ).astype(jnp.bfloat16)
     arrived_part = lax.all_to_all(outgoing, "expert", split_axis=0, concat_axis=0, tiled=True)
-    arrived = lax.all_gather(arrived_part, "tensor", axis=2, tiled=True)
+    arrived = ring_gather(arrived_part, "tensor", 2)
     gate_val = jnp.einsum("gmd,df->gmf", arrived, w_gate[0], preferred_element_type=jnp.float32)
     up_val = jnp.einsum("gmd,df->gmf", arrived, w_up[0], preferred_element_type=jnp.float32)
     returned = finish_slots(gate_val, up_val, w_down[0])

time: 367 us -> 410 us (1.12)
  local copies, waits for them, and re-layouts: 9.17 us -> 42 us
  starting transfers between devices: 9.88 us -> 32.1 us
  waiting for transfers between devices: 233 us -> 219 us
    all_gather x1 -> x0, waiting for transfers between devices: 50.6 us -> none  [on_device(): arrived = lax.all_gather(arrived_part, 'tensor', axis=2, tiled=True)]
    ppermute x0 -> x7, waiting for transfers between devices: none -> 35.3 us  [the longest x4 34.2 us: ring_gather(): lower.append(lax.ppermute(lower[-1] if lower else x, axis, pairs))]
    ppermute x0 -> x7, starting transfers between devices: none -> 22.2 us  [the longest x3 12 us: ring_gather(): upper.append(lax.ppermute(upper[-1] if upper else x, axis, back))]
    unnamed x21 -> x28, local copies, waits for them, and re-layouts: 0.28 us -> 16 us
    reshape x0 -> x1, local copies, waits for them, and re-layouts: none -> 8.05 us  [joined_along(): tiles.reshape(*lengths[:dim], lengths[dim] * lengths[dim + 1], *lengths[d...]
    gather x0 -> x1, local copies, waits for them, and re-layouts: none -> 8.04 us  [ring_gather(): blocks = blocks[(jnp.arange(length) - shift) % length]]
  transfers between devices with their start and end apart: 5 -> 11, of which waited for: 5 -> 10; matrix products, arithmetic and copies ran while one was open for 1% -> 5% of each run, Pallas kernels for 0% -> 0%
where the time goes in v1:
time: 410 us
  waiting for transfers between devices  219 us (53%)
  blocking collectives  66.5 us (16%)
  local copies, waits for them, and re-layouts  42 us (10%)
  starting transfers between devices  32.1 us (8%)
  matrix products  29.1 us (7%)
  between operations  14 us (3%)
  other arithmetic  6.73 us (2%)
    all_gather x1, waiting for transfers between devices, on_device(): all_stream = lax.all_gather(stream, 'expert', axis=0, tiled=True)  72.8 us
    reduce_scatter x1, waiting for transfers between devices, finish_slots(): lax.psum_scatter(partial_out.astype(jnp.bfloat16), 'tensor', scatter_dime...  57.1 us
    all_to_all x1, blocking collectives, on_device(): lax.all_to_all(outgoing, 'expert', split_axis=0, concat_axis=0, tiled=True)  34.5 us
    ppermute x4, waiting for transfers between devices, ring_gather(): lower.append(lax.ppermute(lower[-1] if lower else x, axis, pairs))  34.2 us
    reduce_scatter x1, waiting for transfers between devices, on_device(): lax.psum_scatter(partial_proj.astype(jnp.bfloat16), 'tensor', scatter_dim...  31.4 us
    all_to_all x1, waiting for transfers between devices, finish_slots(): lax.all_to_all(summed, 'expert', split_axis=0, concat_axis=0, tiled=True)  22.5 us
    psum x1, blocking collectives, final_norm(): square_total = lax.psum(jnp.sum(stream_f * stream_f, axis=1), 'tensor')  17.1 us
    dot_general x1, matrix products, finish_slots(): jnp.einsum('gmf,fd->gmd', active, down_weight, preferred_element_type=jnp...  16.8 us
  transfers between devices with their start and end apart: 11, of which 10 were waited for; matrix products, arithmetic and copies ran while one was open for 5% of the time, Pallas kernels for 0%

profile of v1, /device:TPU:1, one launch (start us, length us, event | category | flops | bytes accessed | tf_op | source)
XLA Modules:
  0.0 409.5 jit_solution(16150398641386019278)
XLA Ops:
  7.2 4.0 convolution_convert_fusion.1
  15.5 31.4 %reduce-scatter.3.cloned.1.call-done = bf16[64,512]{1,0:T(8,128)(2,1)} async-done(((bf16[64,4096]{1,0:T(8,128)(2,1)}), bf16[64,512]{1,0:T(8,128)(2,1)}) %reduce-scatter.3.cloned.1.call-update) | async-done | bytes 65552 | tf_op jit(solution)/shard_map/reduce_scatter | solution.py:68
  48.7 14.9 %all-reduce = (f32[64]{0:T(128)S(1)}, f32[64,8]{0,1:T(8,128)S(1)}) all-reduce(f32[64]{0:T(128)S(1)} %get-tuple-element.10, f32[64,8]{0,1:T(8,128)S(1)} %fusion.23), channel_id=1, replica_groups=mesh['expert'=32,'tensor'=8] {'tensor'}, use_global_device_ids=true, to_apply=%region_4.0 | all-reduce | flops 576 | bytes 4608 | tf_op jit(solution)/shard_map/psum | solution.py:74
  64.8 34.5 %all_to_all.10 = bf16[32,32,512]{2,1,0:T(8,128)(2,1)S(1)} all-to-all(bf16[32,32,512]{2,1,0:T(8,128)(2,1)S(1)} %convolution_convert_fusion.2), channel_id=1, replica_groups=mesh['expert'=32,'tensor'=8] {'expert'}, dimensions={0} | all-to-all | bytes 2097152 | tf_op jit(solution)/shard_map/all_to_all | solution.py:103
  99.3 2.7 collective-permute-start
  102.0 11.7 %collective-permute-done = bf16[32,32,512]{2,1,0:T(8,128)(2,1)S(1)} collective-permute-done((bf16[32,32,512]{2,1,0:T(8,128)(2,1)S(1)}, bf16[32,32,512]{2,1,0:T(8,128)(2,1)S(1)}, u32[]{:S(2)}, u32[]{:S(2)}) %collective-permute-start) | collective-permute-done | bytes 1048608 | tf_op jit(solution)/shard_map/ppermute | solution.py:24
  113.8 2.5 collective-permute-start.1
  116.2 3.1 collective-permute-start.4
  119.3 8.6 %collective-permute-done.1 = bf16[32,32,512]{2,1,0:T(8,128)(2,1)S(1)} collective-permute-done((bf16[32,32,512]{2,1,0:T(8,128)(2,1)S(1)}, bf16[32,32,512]{2,1,0:T(8,128)(2,1)S(1)}, u32[]{:S(2)}, u32[]{:S(2)}) %collective-permute-start.1) | collective-permute-done | bytes 1048608 | tf_op jit(solution)/shard_map/ppermute | solution.py:24
  128.0 2.5 collective-permute-start.2
  130.8 4.0 collective-permute-start.5
  134.8 7.4 %collective-permute-done.2 = bf16[32,32,512]{2,1,0:T(8,128)(2,1)} collective-permute-done((bf16[32,32,512]{2,1,0:T(8,128)(2,1)S(1)}, bf16[32,32,512]{2,1,0:T(8,128)(2,1)}, u32[]{:S(2)}, u32[]{:S(2)}) %collective-permute-start.2) | collective-permute-done | bytes 1048608 | tf_op jit(solution)/shard_map/ppermute | solution.py:24
  142.2 2.6 collective-permute-start.3
  145.6 4.9 %collective-permute-start.6 = (bf16[32,32,512]{2,1,0:T(8,128)(2,1)}, bf16[32,32,512]{2,1,0:T(8,128)(2,1)S(1)}, u32[]{:S(2)}, u32[]{:S(2)}) collective-permute-start(bf16[32,32,512]{2,1,0:T(8,128)(2,1)} %collective-permute-done.5), channel_id=1, source_target_pairs={{1,0},{2,1},{3,2},{4,3},{5,4},{6,5},{7,6},{0,7},{9,8},{10,9},{11,1... | collective-permute-start | bytes 3145736 | tf_op jit(solution)/shard_map/ppermute | solution.py:26
  150.5 6.4 %collective-permute-done.3 = bf16[32,32,512]{2,1,0:T(8,128)(2,1)} collective-permute-done((bf16[32,32,512]{2,1,0:T(8,128)(2,1)}, bf16[32,32,512]{2,1,0:T(8,128)(2,1)}, u32[]{:S(2)}, u32[]{:S(2)}) %collective-permute-start.3) | collective-permute-done | bytes 1048608 | tf_op jit(solution)/shard_map/ppermute | solution.py:24
  156.8 2.3 bitcast_dynamic-update-slice_fusion.7
  159.2 2.4 bitcast_dynamic-update-slice_fusion.6
  161.5 2.3 bitcast_dynamic-update-slice_fusion.5
  163.9 2.3 bitcast_dynamic-update-slice_fusion.4
  167.2 2.4 bitcast_dynamic-update-slice_fusion.2
  169.6 2.3 bitcast_dynamic-update-slice_fusion.1
  173.0 8.0 %gather_fusion.2 = bf16[8,32,32,512]{3,2,1,0:T(8,128)(2,1)} fusion(bf16[8,32,32,512]{3,2,1,0:T(8,128)(2,1)} %bitcast_dynamic-update-slice_fusion, s32[1024]{0:T(1024)S(1)} %pad_clamp_fusion.2), kind=kCustom, calls=%fused_computation.2 | custom fusion | bytes 16777248 | tf_op jit(solution)/shard_map/gather | solution.py:29
  181.0 8.1 %copy.94 = bf16[8,32,4,8,512]{4,3,0,2,1:T(8,128)(2,1)} copy(bf16[8,32,4,8,512]{4,3,2,1,0:T(8,128)(2,1)} %bitcast.56) | data formatting | bytes 16777216 | tf_op jit(solution)/shard_map/reshape | solution.py:14
  189.1 5.7 %fusion.3 = f32[32,32,256]{2,1,0:T(8,128)S(1)} fusion(bf16[32,32,4096]{2,1,0:T(8,128)(2,1)} %bitcast.58, bf16[1,4096,256]{2,1,0:T(8,128)(2,1)S(1)} %copy-done.7), kind=kOutput, calls=%fused_computation.10 | convolution fusion | flops 2147483648 | bytes 11534336 | tf_op jit(solution)/shard_map/gmd,df->gmf/dot_general | solution.py:105
  194.8 16.8 %convolution_convert_fusion = bf16[32,32,4096]{2,1,0:T(8,128)(2,1)} fusion(bf16[1,256,4096]{2,1,0:T(8,128)(2,1)S(1)} %copy-done, bf16[32,32,4096]{2,1,0:T(8,128)(2,1)} %bitcast.59, bf16[1,4096,256]{2,1,0:T(8,128)(2,1)} %param.19, f32[32,32,256]{2,1,0:T(8,128)S(1)} %fusion.3), kind=kOutput, calls=%fused_computation.5 | convolution fusion | flops 4300734464 | bytes 22020096 | tf_op jit(solution)/shard_map/gmf,fd->gmd/dot_general | solution.py:35
  211.7 57.1 %reduce-scatter.5.cloned.1.call-done = bf16[32,32,512]{2,1,0:T(8,128)(2,1)} async-done(((bf16[32,32,4096]{2,1,0:T(8,128)(2,1)}), bf16[32,32,512]{2,1,0:T(8,128)(2,1)}) %reduce-scatter.5.cloned.1.call-update) | async-done | bytes 1048592 | tf_op jit(solution)/shard_map/reduce_scatter | solution.py:36
  268.8 9.5 %all-to-all-start.1 = ((bf16[32,32,512]{2,1,0:T(8,128)(2,1)}), bf16[32,32,512]{2,1,0:T(8,128)(2,1)S(1)}, u32[]{:S(2)}, u32[]{:S(2)}) async-start(bf16[32,32,512]{2,1,0:T(8,128)(2,1)} %reduce-scatter.5.cloned.1.call-done), calls=%async_computation.3 | async-start | bytes 2097152 | tf_op jit(solution)/shard_map/all_to_all | solution.py:39
  281.1 22.5 %all-to-all-done.1 = bf16[32,32,512]{2,1,0:T(8,128)(2,1)S(1)} async-done(((bf16[32,32,512]{2,1,0:T(8,128)(2,1)}), bf16[32,32,512]{2,1,0:T(8,128)(2,1)S(1)}, u32[]{:S(2)}, u32[]{:S(2)}) %all-to-all-start.1) | async-done | bytes 1048608 | tf_op jit(solution)/shard_map/all_to_all | solution.py:39
  303.5 2.6 gather_fusion.3
  309.6 72.8 %all-gather.2.cloned.1.call-done = bf16[2048,512]{1,0:T(8,128)(2,1)} async-done(((bf16[64,512]{1,0:T(8,128)(2,1)}), bf16[2048,512]{1,0:T(8,128)(2,1)}) %all-gather.2.cloned.1.call-update) | async-done | bytes 2097168 | tf_op jit(solution)/shard_map/all_gather | solution.py:123
  382.4 2.6 gather_fusion.4
  385.2 17.1 %psum.23 = f32[64]{0:T(128)S(1)} all-reduce(f32[64]{0:T(128)S(1)} %get-tuple-element.4), channel_id=1, replica_groups=mesh['expert'=32,'tensor'=8] {'tensor'}, use_global_device_ids=true, to_apply=%region_14.15 | all-reduce | flops 64 | bytes 512 | tf_op jit(solution)/shard_map/psum | solution.py:44
  (82 shorter events, 17.5 us)
Async XLA Ops:
  7.2 187.7 %copy-start = (bf16[1,256,4096]{2,1,0:T(8,128)(2,1)S(1)}, bf16[1,256,4096]{2,1,0:T(8,128)(2,1)}, u32[]{:S(2)}) copy-start(bf16[1,256,4096]{2,1,0:T(8,128)(2,1)} %param.20) | copy-start | bytes 6291460
  7.2 39.6 %reduce-scatter.3.cloned.1.call-start = ((), (), s32[]{:S(2)}) async-start(), calls=%async_computation.4 | async-start | bytes 589824 | tf_op jit(solution)/shard_map/reduce_scatter | solution.py:68
  11.2 257.6 %reduce-scatter.5.cloned.1.call-start = ((), (), s32[]{:S(2)}) async-start(), calls=%async_computation.5 | async-start | bytes 9437184 | tf_op jit(solution)/shard_map/reduce_scatter | solution.py:36
  99.3 14.4 %collective-permute-start = (bf16[32,32,512]{2,1,0:T(8,128)(2,1)S(1)}, bf16[32,32,512]{2,1,0:T(8,128)(2,1)S(1)}, u32[]{:S(2)}, u32[]{:S(2)}) collective-permute-start(bf16[32,32,512]{2,1,0:T(8,128)(2,1)S(1)} %all_to_all.10), channel_id=1, source_target_pairs={{0,1},{1,2},{2,3},{3,4},{4,5},{5,6},{6,7},{7,0},{8,9},{9,10},{10,1... | collective-permute-start | bytes 3145736 | tf_op jit(solution)/shard_map/ppermute | solution.py:24
  113.7 17.0 %copy-start.1 = (bf16[32,32,512]{2,1,0:T(8,128)(2,1)}, bf16[32,32,512]{2,1,0:T(8,128)(2,1)S(1)}, u32[]{:S(2)}) copy-start(bf16[32,32,512]{2,1,0:T(8,128)(2,1)S(1)} %collective-permute-done) | copy-start | bytes 3145732
  113.8 14.2 %collective-permute-start.1 = (bf16[32,32,512]{2,1,0:T(8,128)(2,1)S(1)}, bf16[32,32,512]{2,1,0:T(8,128)(2,1)S(1)}, u32[]{:S(2)}, u32[]{:S(2)}) collective-permute-start(bf16[32,32,512]{2,1,0:T(8,128)(2,1)S(1)} %collective-permute-done), channel_id=1, source_target_pairs={{0,1},{1,2},{2,3},{3,4},{4,5},{5,6},{6,7},{7,0},{8,9},{9,10},{10,1... | collective-permute-start | bytes 3145736 | tf_op jit(solution)/shard_map/ppermute | solution.py:24
  116.2 14.5 %collective-permute-start.4 = (bf16[32,32,512]{2,1,0:T(8,128)(2,1)S(1)}, bf16[32,32,512]{2,1,0:T(8,128)(2,1)}, u32[]{:S(2)}, u32[]{:S(2)}) collective-permute-start(bf16[32,32,512]{2,1,0:T(8,128)(2,1)S(1)} %all_to_all.10), channel_id=1, source_target_pairs={{1,0},{2,1},{3,2},{4,3},{5,4},{6,5},{7,6},{0,7},{9,8},{10,9},{11,1... | collective-permute-start | bytes 3145736 | tf_op jit(solution)/shard_map/ppermute | solution.py:26
  128.0 6.8 %copy-start.2 = (bf16[32,32,512]{2,1,0:T(8,128)(2,1)}, bf16[32,32,512]{2,1,0:T(8,128)(2,1)S(1)}, u32[]{:S(2)}) copy-start(bf16[32,32,512]{2,1,0:T(8,128)(2,1)S(1)} %collective-permute-done.1) | copy-start | bytes 3145732
  128.0 14.2 %collective-permute-start.2 = (bf16[32,32,512]{2,1,0:T(8,128)(2,1)S(1)}, bf16[32,32,512]{2,1,0:T(8,128)(2,1)}, u32[]{:S(2)}, u32[]{:S(2)}) collective-permute-start(bf16[32,32,512]{2,1,0:T(8,128)(2,1)S(1)} %collective-permute-done.1), channel_id=1, source_target_pairs={{0,1},{1,2},{2,3},{3,4},{4,5},{5,6},{6,7},{7,0},{8,9},{9,10},{10,1... | collective-permute-start | bytes 3145736 | tf_op jit(solution)/shard_map/ppermute | solution.py:24
  130.8 14.8 %collective-permute-start.5 = (bf16[32,32,512]{2,1,0:T(8,128)(2,1)}, bf16[32,32,512]{2,1,0:T(8,128)(2,1)}, u32[]{:S(2)}, u32[]{:S(2)}) collective-permute-start(bf16[32,32,512]{2,1,0:T(8,128)(2,1)} %collective-permute-done.4), channel_id=1, source_target_pairs={{1,0},{2,1},{3,2},{4,3},{5,4},{6,5},{7,6},{0,7},{9,8},{10,9},{11,1... | collective-permute-start | bytes 3145736 | tf_op jit(solution)/shard_map/ppermute | solution.py:26
  142.2 14.6 %collective-permute-start.3 = (bf16[32,32,512]{2,1,0:T(8,128)(2,1)}, bf16[32,32,512]{2,1,0:T(8,128)(2,1)}, u32[]{:S(2)}, u32[]{:S(2)}) collective-permute-start(bf16[32,32,512]{2,1,0:T(8,128)(2,1)} %collective-permute-done.2), channel_id=1, source_target_pairs={{0,1},{1,2},{2,3},{3,4},{4,5},{5,6},{6,7},{7,0},{8,9},{9,10},{10,1... | collective-permute-start | bytes 3145736 | tf_op jit(solution)/shard_map/ppermute | solution.py:24
  145.6 26.3 %collective-permute-start.6 = (bf16[32,32,512]{2,1,0:T(8,128)(2,1)}, bf16[32,32,512]{2,1,0:T(8,128)(2,1)S(1)}, u32[]{:S(2)}, u32[]{:S(2)}) collective-permute-start(bf16[32,32,512]{2,1,0:T(8,128)(2,1)} %collective-permute-done.5), channel_id=1, source_target_pairs={{1,0},{2,1},{3,2},{4,3},{5,4},{6,5},{7,6},{0,7},{9,8},{10,9},{11,1... | collective-permute-start | bytes 3145736 | tf_op jit(solution)/shard_map/ppermute | solution.py:26
  181.0 8.1 %copy-start.7 = (bf16[1,4096,256]{2,1,0:T(8,128)(2,1)S(1)}, bf16[1,4096,256]{2,1,0:T(8,128)(2,1)}, u32[]{:S(2)}) copy-start(bf16[1,4096,256]{2,1,0:T(8,128)(2,1)} %param.18) | copy-start | bytes 6291460
  211.6 67.0 %copy-start.5 = (s32[64,2]{0,1:T(2,128)S(1)}, s32[64,2]{0,1:T(2,128)}, u32[]{:S(2)}) copy-start(s32[64,2]{0,1:T(2,128)} %param.17) | copy-start | bytes 1540
  211.6 67.3 %copy-start.8 = (s32[32]{0:T(128)S(1)}, s32[32]{0:T(128)}, u32[]{:S(2)}) copy-start(s32[32]{0:T(128)} %param.21) | copy-start | bytes 388
  211.6 97.7 %copy-start.4 = (s32[2048]{0:T(1024)S(1)}, s32[2048]{0:T(1024)}, u32[]{:S(2)}) copy-start(s32[2048]{0:T(1024)} %param.23) | copy-start | bytes 24580
  211.6 190.6 %copy-start.6 = (f32[512]{0:T(512)S(1)}, f32[512]{0:T(512)}, u32[]{:S(2)}) copy-start(f32[512]{0:T(512)} %param.22) | copy-start | bytes 6148
  268.8 34.7 %all-to-all-start.1 = ((bf16[32,32,512]{2,1,0:T(8,128)(2,1)}), bf16[32,32,512]{2,1,0:T(8,128)(2,1)S(1)}, u32[]{:S(2)}, u32[]{:S(2)}) async-start(bf16[32,32,512]{2,1,0:T(8,128)(2,1)} %reduce-scatter.5.cloned.1.call-done), calls=%async_computation.3 | async-start | bytes 2097152 | tf_op jit(solution)/shard_map/all_to_all | solution.py:39
  278.4 104.0 %all-gather.2.cloned.1.call-start = ((), (), s32[]{:S(2)}) async-start(), calls=%async_computation.6 | async-start | bytes 2162688 | tf_op jit(solution)/shard_map/all_gather | solution.py:123
  385.2 17.8 %copy-start.3 = (bf16[64,512]{1,0:T(8,128)(2,1)}, bf16[64,512]{1,0:T(8,128)(2,1)S(1)}, u32[]{:S(2)}) copy-start(bf16[64,512]{1,0:T(8,128)(2,1)S(1)} %get-tuple-element.5) | copy-start | bytes 196612
Sparse Core Ops, SparseCore 0:
  11.4 35.4 reduce-scatter.2
  211.8 56.9 reduce-scatter.4
  309.4 72.9 all-gather.1
